TPU v7x, 256 devices: a whole 4x4x8 slice. The times are simulated.
256 devices in a mesh: ctx: 32 (over y, z), tp: 8 (over x, core).
Axes of the slice: x: 4, y: 4, z: 8, core: 2. Of those that a mesh axis runs over, the one named last changes fastest.
Arguments:
- tokens: bfloat16 [16384, 4096], P('ctx', 'tp'), may hold values from -6 to 6
- qkv_blocks: bfloat16 [3, 4, 1024, 1024], P(None, None, None, 'tp'), may hold values from -0.046875 to 0.046875
- out_blocks: bfloat16 [4, 1024, 1024], P(None, 'tp'), may hold values from -0.046875 to 0.046875
- mix_factors: float32 [4, 4, 4, 4], replicated, may hold values from -4 to 4
- head_gain: float32 [4, 1024], P(None, 'tp'), may hold values from 0.1 to 1.9
Outputs:
- layer_out: bfloat16 [16384, 4096], P('ctx', 'tp')
All inputs are finite; a program needn't handle non-finite values.
Results may differ from a plain program's by a relative error of at most 0.025.
Values may be sent and summed in bfloat16 or wider, within the bound.
No kernel may reach another device: no remote copies, remote signals or barrier semaphores. Data moves between devices by JAX's collectives and lax.ppermute only.
A program may use at most 128 MiB of HBM per device.

v0:
```python
import functools
import jax
import jax.numpy as jnp
from jax import lax
from jax.sharding import PartitionSpec as P

PHM = 4
SPAN = 128
HEAD = 128
BLOCK = 1024
epsilon = 1e-06


def ring_gather(value, axis, devices, size, stride, before):
    here = lax.axis_index(axis)
    k_here = here // stride % size
    total = value.astype(jnp.float32)
    earlier = jnp.zeros_like(total)
    for shift in range(1, size):
        pairs = []
        for i in range(devices):
            k = i // stride % size
            pairs.append((i, i + ((k + shift) % size - k) * stride))
        got = lax.ppermute(value, axis, pairs).astype(jnp.float32)
        source = (k_here - shift) % size
        total = total + got
        earlier = earlier + jnp.where(source < before, got, 0.0)
    return (total, earlier)


def exclusive_prefix(value, axis, devices, row):
    here = lax.axis_index(axis)
    pos, col = (here % row, here // row)
    row_total, before = ring_gather(value.astype(jnp.bfloat16), axis, devices, row, 1, pos)
    _, rows_before = ring_gather(row_total, axis, devices, devices // row, row, col)
    return before + rows_before


def fold_weights(blocks, mixing):
    terms, rows, cols = blocks.shape
    folded = None
    for term_index in range(terms):
        part = (
            mixing[term_index][:, None, :, None]
            * blocks[term_index].astype(jnp.float32)[None, :, None, :]
        )
        folded = part if folded is None else folded + part
    return folded.reshape(PHM * rows, PHM * cols)


def project(whole, blocks, mixing):
    projections, terms, rows, cols = blocks.shape
    tok_rows = whole.shape[0]
    weights = jnp.transpose(blocks, (2, 0, 1, 3)).reshape(rows, projections * terms * cols)
    products = [
        jnp.dot(whole[:, c * rows : (c + 1) * rows], weights, preferred_element_type=jnp.float32)
        for c in range(PHM)
    ]
    outs = []
    for p in range(projections):
        blocks_out = []
        for r in range(PHM):
            summed = None
            for term_index in range(terms):
                at = (p * terms + term_index) * cols
                for c in range(PHM):
                    part = products[c][:, at : at + cols] * mixing[p, term_index, c, r]
                    summed = part if summed is None else summed + part
            blocks_out.append(summed.astype(jnp.bfloat16))
        outs.append(jnp.concatenate(blocks_out, axis=1))
    return lax.optimization_barrier(outs)


def on_device(ctx_devices, ctx_row, tokens, qkv_blocks, out_blocks, mix_factors, head_gain):
    col_width = qkv_blocks.shape[-1]
    w_out = fold_weights(out_blocks, mix_factors[3]).astype(jnp.bfloat16)
    whole = lax.all_gather(tokens, "tp", axis=1, tiled=True)
    tok_rows = whole.shape[0]
    local_heads = PHM * col_width // HEAD
    nblk = tok_rows // SPAN
    width = PHM * col_width
    key, value = project(whole, qkv_blocks[1:], mix_factors[1:3])
    key_heads = key.reshape(nblk, SPAN, local_heads, HEAD)
    value_heads = value.reshape(nblk, SPAN, local_heads, HEAD)
    states = jnp.einsum(
        "nshd,nshe->nhde", key_heads, value_heads, preferred_element_type=jnp.float32
    )
    totals = jnp.sum(states, axis=0)
    earlier_sum = exclusive_prefix(totals, "ctx", ctx_devices, ctx_row)
    (query,) = project(whole, qkv_blocks[:1], mix_factors[:1])
    query_heads = query.reshape(nblk, SPAN, local_heads, HEAD)
    scores = jnp.einsum(
        "nshd,nthd->nhst", query_heads, key_heads, preferred_element_type=jnp.float32
    )
    causal = jnp.arange(SPAN)[:, None] >= jnp.arange(SPAN)[None, :]
    scores = jnp.where(causal[None, None], scores, 0.0).astype(jnp.bfloat16)
    within = jnp.einsum("nhst,nthe->nshe", scores, value_heads, preferred_element_type=jnp.float32)
    prefixes = [earlier_sum]
    for n in range(1, nblk):
        prefixes.append(prefixes[-1] + states[n - 1])
    prefix = jnp.stack(prefixes, axis=0)
    prefix_hi = prefix.astype(jnp.bfloat16)
    prefix_lo = (prefix - prefix_hi.astype(jnp.float32)).astype(jnp.bfloat16)
    carried_out = jnp.einsum(
        "nshd,nhde->nshe",
        jnp.concatenate([query_heads, query_heads], axis=-1),
        jnp.concatenate([prefix_hi, prefix_lo], axis=-2),
        preferred_element_type=jnp.float32,
    )
    combined = within + carried_out
    mean_sq = jnp.mean(combined * combined, axis=-1, keepdims=True)
    normed = combined * lax.rsqrt(mean_sq + epsilon) * head_gain
    attn = normed.astype(jnp.bfloat16).reshape(tok_rows, PHM * col_width)
    partial_value = jnp.dot(attn, w_out, preferred_element_type=jnp.float32)
    reduced = lax.psum_scatter(
        partial_value.astype(jnp.bfloat16), "tp", scatter_dimension=1, tiled=True
    )
    return reduced


def ctx_row_of(mesh):
    n = mesh.shape["ctx"]
    return 8 if n % 8 == 0 else n


def solution(mesh):
    placed = (P("ctx", "tp"), P(None, None, None, "tp"), P(None, "tp", None), P(), P(None, "tp"))
    return jax.shard_map(
        functools.partial(on_device, mesh.shape["ctx"], ctx_row_of(mesh)),
        mesh=mesh,
        in_specs=placed,
        out_specs=P("ctx", "tp"),
        check_vma=False,
    )
```

profile of v0, /device:TPU:8, one launch (start us, length us, event | category | flops | bytes accessed | tf_op | source)
XLA Modules:
  0.0 269.7 jit_solution(15784364006472150208)
XLA Ops:
  6.5 0.7 all-gather.2.cloned.1.call-update
  7.5 1.6 slice-done
  9.1 2.7 copy.22
  11.8 1.3 copy.23
  13.1 0.2 bitcast_convert_fusion.3
  13.3 4.8 %add_convert_fusion = bf16[4,128,4,1024]{3,2,1,0:T(4,128)(2,1)S(1)} fusion(f32[128,1024]{1,0:T(8,128)S(1)} %get-tuple-element.15, f32[4,4]{1,0:T(4,128)S(1)} %get-tuple-element.212, f32[128,1024]{1,0:T(8,128)S(1)} %get-tuple-element.16, f32[4,4]{1,0:T(4,128)S(1)} %get-tuple-element.211, f32[128,1024]{1,0:T(8,128)S(1)} %get-tuple-element.14, ...), kind=kLoop, calls=%fused_computation | loop fusion | flops 16777216 | bytes 6291712 | tf_op jit(solution)/shard_map/convert_element_type | solution.py:76
  18.1 4.3 %copy.25 = bf16[64,8,4,1024]{3,1,2,0:T(8,128)(2,1)} copy(bf16[64,8,4,1024]{3,2,1,0:T(4,128)(2,1)S(1)} %bitcast.275) | data formatting | bytes 8388608
  22.5 0.6 fusion.59
  23.1 0.6 fusion.57
  23.7 0.7 fusion.55
  24.4 0.7 fusion.56
  25.1 0.7 fusion.49
  25.9 0.7 fusion.53
  26.6 0.7 fusion.54
  27.3 0.7 fusion.50
  28.1 0.7 fusion.51
  28.8 0.7 fusion.52
  29.5 0.7 fusion.58
  30.2 16.5 %all-gather.2.cloned.1.call-done = bf16[512,4096]{1,0:T(8,128)(2,1)} async-done(((bf16[512,512]{1,0:T(8,128)(2,1)}), bf16[512,4096]{1,0:T(8,128)(2,1)}) %all-gather.2.cloned.1.call-update) | async-done | bytes 4194320 | tf_op jit(solution)/shard_map/all_gather | solution.py:77
  46.7 2.7 fusion.11
  49.3 1.3 fusion.15
  50.6 1.3 fusion.19
  51.9 1.3 fusion.23
  53.2 9.7 %add_convert_fusion.10 = bf16[512,128]{1,0:T(8,128)(2,1)S(1)} fusion(f32[512,1024]{1,0:T(8,128)S(1)} %fusion.11, f32[512,1024]{1,0:T(8,128)S(1)} %fusion.15, f32[512,1024]{1,0:T(8,128)S(1)} %fusion.19, f32[512,1024]{1,0:T(8,128)S(1)} %fusion.23, f32[]{:T(128)} %bitcast.50, f32[]{:T(128)} %bitcast.49, f32[]{:T(128)} %bitcast.48, f32[]{:T(128)} %bitcast.47, ...), kind=kLoop, calls=%fused_computation.85 | loop fusion | flops 2097152 | bytes 4325440 | tf_op jit(solution)/shard_map/convert_element_type | solution.py:69
  63.0 10.2 %add_convert_fusion.11 = bf16[512,128]{1,0:T(8,128)(2,1)S(1)} fusion(f32[512,1024]{1,0:T(8,128)S(1)} %fusion.11, f32[512,1024]{1,0:T(8,128)S(1)} %fusion.15, f32[512,1024]{1,0:T(8,128)S(1)} %fusion.19, f32[512,1024]{1,0:T(8,128)S(1)} %fusion.23, f32[]{:T(128)} %bitcast.34, f32[]{:T(128)} %bitcast.33, f32[]{:T(128)} %bitcast.32, f32[]{:T(128)} %bitcast.31, ...), kind=kLoop, calls=%fused_computation.86 | loop fusion | flops 2097152 | bytes 4325440 | tf_op jit(solution)/shard_map/convert_element_type | solution.py:69
  73.2 10.3 %add_convert_fusion.5 = bf16[512,128]{1,0:T(8,128)(2,1)S(1)} fusion(f32[512,1024]{1,0:T(8,128)S(1)} %fusion.11, f32[512,1024]{1,0:T(8,128)S(1)} %fusion.15, f32[512,1024]{1,0:T(8,128)S(1)} %fusion.19, f32[512,1024]{1,0:T(8,128)S(1)} %fusion.23, f32[]{:T(128)} %bitcast.130, f32[]{:T(128)} %bitcast.129, f32[]{:T(128)} %bitcast.128, f32[]{:T(128)} %bitcast.127, ...), kind=kLoop, calls=%fused_computation.80 | loop fusion | flops 2097152 | bytes 4325440 | tf_op jit(solution)/shard_map/convert_element_type | solution.py:69
  83.5 10.5 %add_convert_fusion.6 = bf16[512,128]{1,0:T(8,128)(2,1)S(1)} fusion(f32[512,1024]{1,0:T(8,128)S(1)} %fusion.11, f32[512,1024]{1,0:T(8,128)S(1)} %fusion.15, f32[512,1024]{1,0:T(8,128)S(1)} %fusion.19, f32[512,1024]{1,0:T(8,128)S(1)} %fusion.23, f32[]{:T(128)} %bitcast.114, f32[]{:T(128)} %bitcast.113, f32[]{:T(128)} %bitcast.112, f32[]{:T(128)} %bitcast.111, ...), kind=kLoop, calls=%fused_computation.81 | loop fusion | flops 2097152 | bytes 4325440 | tf_op jit(solution)/shard_map/convert_element_type | solution.py:69
  94.1 10.3 %add_convert_fusion.7 = bf16[512,128]{1,0:T(8,128)(2,1)S(1)} fusion(f32[512,1024]{1,0:T(8,128)S(1)} %fusion.11, f32[512,1024]{1,0:T(8,128)S(1)} %fusion.15, f32[512,1024]{1,0:T(8,128)S(1)} %fusion.19, f32[512,1024]{1,0:T(8,128)S(1)} %fusion.23, f32[]{:T(128)} %bitcast.98, f32[]{:T(128)} %bitcast.97, f32[]{:T(128)} %bitcast.96, f32[]{:T(128)} %bitcast.95, ...), kind=kLoop, calls=%fused_computation.82 | loop fusion | flops 2097152 | bytes 4325440 | tf_op jit(solution)/shard_map/convert_element_type | solution.py:69
  104.4 10.4 %add_convert_fusion.8 = bf16[512,128]{1,0:T(8,128)(2,1)S(1)} fusion(f32[512,1024]{1,0:T(8,128)S(1)} %fusion.11, f32[512,1024]{1,0:T(8,128)S(1)} %fusion.15, f32[512,1024]{1,0:T(8,128)S(1)} %fusion.19, f32[512,1024]{1,0:T(8,128)S(1)} %fusion.23, f32[]{:T(128)} %bitcast.82, f32[]{:T(128)} %bitcast.81, f32[]{:T(128)} %bitcast.80, f32[]{:T(128)} %bitcast.79, ...), kind=kLoop, calls=%fused_computation.83 | loop fusion | flops 2097152 | bytes 4325440 | tf_op jit(solution)/shard_map/convert_element_type | solution.py:69
  114.8 10.5 %add_convert_fusion.9 = bf16[512,128]{1,0:T(8,128)(2,1)S(1)} fusion(f32[512,1024]{1,0:T(8,128)S(1)} %fusion.11, f32[512,1024]{1,0:T(8,128)S(1)} %fusion.15, f32[512,1024]{1,0:T(8,128)S(1)} %fusion.19, f32[512,1024]{1,0:T(8,128)S(1)} %fusion.23, f32[]{:T(128)} %bitcast.66, f32[]{:T(128)} %bitcast.65, f32[]{:T(128)} %bitcast.64, f32[]{:T(128)} %bitcast.63, ...), kind=kLoop, calls=%fused_computation.84 | loop fusion | flops 2097152 | bytes 4325440 | tf_op jit(solution)/shard_map/convert_element_type | solution.py:69
  125.3 9.9 %add_convert_fusion.12 = bf16[512,128]{1,0:T(8,128)(2,1)S(1)} fusion(f32[512,1024]{1,0:T(8,128)S(1)} %fusion.11, f32[512,1024]{1,0:T(8,128)S(1)} %fusion.15, f32[512,1024]{1,0:T(8,128)S(1)} %fusion.19, f32[512,1024]{1,0:T(8,128)S(1)} %fusion.23, f32[]{:T(128)} %bitcast.18, f32[]{:T(128)} %bitcast.17, f32[]{:T(128)} %bitcast.16, f32[]{:T(128)} %bitcast.15, ...), kind=kLoop, calls=%fused_computation.87 | loop fusion | flops 2097152 | bytes 4325440 | tf_op jit(solution)/shard_map/convert_element_type | solution.py:69
  135.5 0.3 copy.15
  135.9 1.0 fusion.60
  136.9 1.6 collective-permute-start
  138.5 2.5 collective-permute-start.1
  141.0 2.9 %collective-permute-start.2 = (bf16[4,128,128]{2,1,0:T(8,128)(2,1)}, bf16[4,128,128]{2,1,0:T(8,128)(2,1)S(1)}, u32[]{:S(2)}, u32[]{:S(2)}) collective-permute-start(bf16[4,128,128]{2,1,0:T(8,128)(2,1)} %get-tuple-element.213), channel_id=1, source_target_pairs={{0,24},{8,32},{16,40},{24,48},{32,56},{40,0},{48,8},{56,16},{64,88... | collective-permute-start | bytes 393224 | tf_op jit(solution)/shard_map/ppermute | solution.py:24
  144.0 2.0 collective-permute-start.3
  145.9 3.1 %collective-permute-start.4 = (bf16[4,128,128]{2,1,0:T(8,128)(2,1)}, bf16[4,128,128]{2,1,0:T(8,128)(2,1)}, u32[]{:S(2)}, u32[]{:S(2)}) collective-permute-start(bf16[4,128,128]{2,1,0:T(8,128)(2,1)} %get-tuple-element.213), channel_id=1, source_target_pairs={{0,40},{8,48},{16,56},{24,0},{32,8},{40,16},{48,24},{56,32},{64,10... | collective-permute-start | bytes 393224 | tf_op jit(solution)/shard_map/ppermute | solution.py:24
  149.1 2.0 fusion.13
  151.1 0.7 fusion.17
  151.8 0.7 fusion.21
  152.6 0.7 fusion.9
  153.3 10.5 %add_convert_fusion.1 = bf16[512,128]{0,1:T(8,128)(2,1)S(1)} fusion(f32[512,512]{0,1:T(8,128)S(1)} %fusion.9, f32[512,512]{0,1:T(8,128)S(1)} %fusion.13, f32[512,512]{0,1:T(8,128)S(1)} %fusion.17, f32[512,512]{0,1:T(8,128)S(1)} %fusion.21, f32[]{:T(128)} %bitcast.197, f32[]{:T(128)} %bitcast.196, f32[]{:T(128)} %bitcast.195, f32[]{:T(128)} %bitcast.194, ...), kind=kLoop, calls=%fused_computation.76 | loop fusion | flops 2097152 | bytes 4325440 | tf_op jit(solution)/shard_map/convert_element_type | solution.py:69
  163.8 10.4 %add_convert_fusion.2 = bf16[512,128]{0,1:T(8,128)(2,1)S(1)} fusion(f32[512,512]{0,1:T(8,128)S(1)} %fusion.9, f32[512,512]{0,1:T(8,128)S(1)} %fusion.13, f32[512,512]{0,1:T(8,128)S(1)} %fusion.17, f32[512,512]{0,1:T(8,128)S(1)} %fusion.21, f32[]{:T(128)} %bitcast.181, f32[]{:T(128)} %bitcast.180, f32[]{:T(128)} %bitcast.179, f32[]{:T(128)} %bitcast.178, ...), kind=kLoop, calls=%fused_computation.77 | loop fusion | flops 2097152 | bytes 4325440 | tf_op jit(solution)/shard_map/convert_element_type | solution.py:69
  174.2 10.5 %add_convert_fusion.3 = bf16[512,128]{0,1:T(8,128)(2,1)S(1)} fusion(f32[512,512]{0,1:T(8,128)S(1)} %fusion.9, f32[512,512]{0,1:T(8,128)S(1)} %fusion.13, f32[512,512]{0,1:T(8,128)S(1)} %fusion.17, f32[512,512]{0,1:T(8,128)S(1)} %fusion.21, f32[]{:T(128)} %bitcast.165, f32[]{:T(128)} %bitcast.164, f32[]{:T(128)} %bitcast.163, f32[]{:T(128)} %bitcast.162, ...), kind=kLoop, calls=%fused_computation.78 | loop fusion | flops 2097152 | bytes 4325440 | tf_op jit(solution)/shard_map/convert_element_type | solution.py:69
  184.7 3.5 %collective-permute-start.5 = (bf16[4,128,128]{2,1,0:T(8,128)(2,1)}, bf16[4,128,128]{2,1,0:T(8,128)(2,1)}, u32[]{:S(2)}, u32[]{:S(2)}) collective-permute-start(bf16[4,128,128]{2,1,0:T(8,128)(2,1)} %get-tuple-element.213), channel_id=1, source_target_pairs={{0,48},{8,56},{16,0},{24,8},{32,16},{40,24},{48,32},{56,40},{64,11... | collective-permute-start | bytes 393224 | tf_op jit(solution)/shard_map/ppermute | solution.py:24
  188.2 1.4 collective-permute-start.6
  189.6 10.5 %add_convert_fusion.4 = bf16[512,128]{0,1:T(8,128)(2,1)S(1)} fusion(f32[512,512]{0,1:T(8,128)S(1)} %fusion.9, f32[512,512]{0,1:T(8,128)S(1)} %fusion.13, f32[512,512]{0,1:T(8,128)S(1)} %fusion.17, f32[512,512]{0,1:T(8,128)S(1)} %fusion.21, f32[]{:T(128)} %bitcast.149, f32[]{:T(128)} %bitcast.148, f32[]{:T(128)} %bitcast.147, f32[]{:T(128)} %bitcast.146, ...), kind=kLoop, calls=%fused_computation.79 | loop fusion | flops 2097152 | bytes 4325440 | tf_op jit(solution)/shard_map/convert_element_type | solution.py:69
  200.3 0.4 copy.18
  200.7 2.0 convert_add_fusion
  202.7 1.5 collective-permute-start.7
  204.2 1.1 collective-permute-start.8
  205.3 2.1 collective-permute-start.9
  207.5 1.6 fusion.2
  209.1 3.0 %collective-permute-done.7 = f32[4,128,128]{2,1,0:T(8,128)S(1)} collective-permute-done((f32[4,128,128]{2,1,0:T(8,128)}, f32[4,128,128]{2,1,0:T(8,128)S(1)}, u32[]{:S(2)}, u32[]{:S(2)}) %collective-permute-start.7) | collective-permute-done | bytes 262176 | tf_op jit(solution)/shard_map/ppermute | solution.py:24
  212.1 2.9 %collective-permute-done.8 = f32[4,128,128]{2,1,0:T(8,128)S(1)} collective-permute-done((f32[4,128,128]{2,1,0:T(8,128)}, f32[4,128,128]{2,1,0:T(8,128)S(1)}, u32[]{:S(2)}, u32[]{:S(2)}) %collective-permute-start.8) | collective-permute-done | bytes 262176 | tf_op jit(solution)/shard_map/ppermute | solution.py:24
  215.0 2.2 collective-permute-done.9
  217.2 1.3 fusion.44
  218.8 0.9 copy-done.3
  219.7 0.5 multiply_reduce_fusion
  220.4 0.2 multiply_convert_fusion
  220.6 0.3 copy.20
  220.9 6.6 %convolution_convert_fusion = bf16[512,4096]{1,0:T(8,128)(2,1)} fusion(bf16[512,4096]{1,0:T(8,128)(2,1)} %bitcast.276, bf16[64,8,4,128]{3,2,1,0:T(4,128)(2,1)S(1)} %bitcast.287), kind=kOutput, calls=%fused_computation.1 | convolution fusion | flops 2149580800 | bytes 8912896 | tf_op jit(solution)/shard_map/dot_general | solution.py:114
  227.5 35.3 %reduce-scatter.2.cloned.1.call-done = bf16[512,512]{1,0:T(8,128)(2,1)} async-done(((bf16[512,4096]{1,0:T(8,128)(2,1)}), bf16[512,512]{1,0:T(8,128)(2,1)}) %reduce-scatter.2.cloned.1.call-update) | async-done | bytes 524304 | tf_op jit(solution)/shard_map/reduce_scatter | solution.py:115
  (39 shorter events, 1.1 us)
Async XLA Ops:
  6.5 40.1 %all-gather.2.cloned.1.call-start = ((), (), s32[]{:S(2)}) async-start(), calls=%async_computation.1 | async-start | bytes 4718592 | tf_op jit(solution)/shard_map/all_gather | solution.py:77
  7.3 255.6 %reduce-scatter.2.cloned.1.call-start = ((), (), s32[]{:S(2)}) async-start(), calls=%async_computation.2 | async-start | bytes 4718592 | tf_op jit(solution)/shard_map/reduce_scatter | solution.py:115
  7.5 1.6 slice-start
  9.1 2.7 slice-start.1
  11.8 1.3 copy-start.4
  11.8 1.3 copy-start.1
  18.1 28.5 %copy-start = (bf16[2,4,1024,128]{2,3,1,0:T(8,128)(2,1)S(1)}, bf16[2,4,1024,128]{2,3,1,0:T(8,128)(2,1)}, u32[]{:S(2)}) copy-start(bf16[2,4,1024,128]{2,3,1,0:T(8,128)(2,1)} %copy.22) | copy-start | bytes 6291460
  46.7 2.7 copy-start.6
  135.5 13.6 %copy-start.2 = (bf16[1,4,1024,128]{2,3,1,0:T(8,128)(2,1)S(1)}, bf16[1,4,1024,128]{2,3,1,0:T(8,128)(2,1)}, u32[]{:S(2)}) copy-start(bf16[1,4,1024,128]{2,3,1,0:T(8,128)(2,1)} %copy.23) | copy-start | bytes 3145732
  135.9 15.1 %copy-start.7 = (bf16[512,4096]{1,0:T(8,128)(2,1)S(1)}, bf16[512,4096]{1,0:T(8,128)(2,1)}, u32[]{:S(2)}) copy-start(bf16[512,4096]{1,0:T(8,128)(2,1)} %all-gather.2.cloned.1.call-done) | copy-start | bytes 12582916
  136.9 47.8 %collective-permute-start = (bf16[4,128,128]{2,1,0:T(8,128)(2,1)}, bf16[4,128,128]{2,1,0:T(8,128)(2,1)S(1)}, u32[]{:S(2)}, u32[]{:S(2)}) collective-permute-start(bf16[4,128,128]{2,1,0:T(8,128)(2,1)} %get-tuple-element.213), channel_id=1, source_target_pairs={{0,8},{8,16},{16,24},{24,32},{32,40},{40,48},{48,56},{56,0},{64,72... | collective-permute-start | bytes 393224 | tf_op jit(solution)/shard_map/ppermute | solution.py:24
  138.5 49.7 %collective-permute-start.1 = (bf16[4,128,128]{2,1,0:T(8,128)(2,1)}, bf16[4,128,128]{2,1,0:T(8,128)(2,1)S(1)}, u32[]{:S(2)}, u32[]{:S(2)}) collective-permute-start(bf16[4,128,128]{2,1,0:T(8,128)(2,1)} %get-tuple-element.213), channel_id=1, source_target_pairs={{0,16},{8,24},{16,32},{24,40},{32,48},{40,56},{48,0},{56,8},{64,80... | collective-permute-start | bytes 393224 | tf_op jit(solution)/shard_map/ppermute | solution.py:24
  141.0 59.7 %collective-permute-start.2 = (bf16[4,128,128]{2,1,0:T(8,128)(2,1)}, bf16[4,128,128]{2,1,0:T(8,128)(2,1)S(1)}, u32[]{:S(2)}, u32[]{:S(2)}) collective-permute-start(bf16[4,128,128]{2,1,0:T(8,128)(2,1)} %get-tuple-element.213), channel_id=1, source_target_pairs={{0,24},{8,32},{16,40},{24,48},{32,56},{40,0},{48,8},{56,16},{64,88... | collective-permute-start | bytes 393224 | tf_op jit(solution)/shard_map/ppermute | solution.py:24
  144.0 56.7 %collective-permute-start.3 = (bf16[4,128,128]{2,1,0:T(8,128)(2,1)}, bf16[4,128,128]{2,1,0:T(8,128)(2,1)}, u32[]{:S(2)}, u32[]{:S(2)}) collective-permute-start(bf16[4,128,128]{2,1,0:T(8,128)(2,1)} %get-tuple-element.213), channel_id=1, source_target_pairs={{0,32},{8,40},{16,48},{24,56},{32,0},{40,8},{48,16},{56,24},{64,96... | collective-permute-start | bytes 393224 | tf_op jit(solution)/shard_map/ppermute | solution.py:24
  145.9 54.7 %collective-permute-start.4 = (bf16[4,128,128]{2,1,0:T(8,128)(2,1)}, bf16[4,128,128]{2,1,0:T(8,128)(2,1)}, u32[]{:S(2)}, u32[]{:S(2)}) collective-permute-start(bf16[4,128,128]{2,1,0:T(8,128)(2,1)} %get-tuple-element.213), channel_id=1, source_target_pairs={{0,40},{8,48},{16,56},{24,0},{32,8},{40,16},{48,24},{56,32},{64,10... | collective-permute-start | bytes 393224 | tf_op jit(solution)/shard_map/ppermute | solution.py:24
  184.7 16.0 %collective-permute-start.5 = (bf16[4,128,128]{2,1,0:T(8,128)(2,1)}, bf16[4,128,128]{2,1,0:T(8,128)(2,1)}, u32[]{:S(2)}, u32[]{:S(2)}) collective-permute-start(bf16[4,128,128]{2,1,0:T(8,128)(2,1)} %get-tuple-element.213), channel_id=1, source_target_pairs={{0,48},{8,56},{16,0},{24,8},{32,16},{40,24},{48,32},{56,40},{64,11... | collective-permute-start | bytes 393224 | tf_op jit(solution)/shard_map/ppermute | solution.py:24
  188.2 12.5 %collective-permute-start.6 = (bf16[4,128,128]{2,1,0:T(8,128)(2,1)}, bf16[4,128,128]{2,1,0:T(8,128)(2,1)}, u32[]{:S(2)}, u32[]{:S(2)}) collective-permute-start(bf16[4,128,128]{2,1,0:T(8,128)(2,1)} %get-tuple-element.213), channel_id=1, source_target_pairs={{0,56},{8,0},{16,8},{24,16},{32,24},{40,32},{48,40},{56,48},{64,12... | collective-permute-start | bytes 393224 | tf_op jit(solution)/shard_map/ppermute | solution.py:24
  202.7 9.4 %collective-permute-start.7 = (f32[4,128,128]{2,1,0:T(8,128)}, f32[4,128,128]{2,1,0:T(8,128)S(1)}, u32[]{:S(2)}, u32[]{:S(2)}) collective-permute-start(f32[4,128,128]{2,1,0:T(8,128)} %convert_add_fusion), channel_id=1, source_target_pairs={{0,64},{8,72},{16,80},{24,88},{32,96},{40,104},{48,112},{56,120},{... | collective-permute-start | bytes 786440 | tf_op jit(solution)/shard_map/ppermute | solution.py:24
  204.2 10.8 %collective-permute-start.8 = (f32[4,128,128]{2,1,0:T(8,128)}, f32[4,128,128]{2,1,0:T(8,128)S(1)}, u32[]{:S(2)}, u32[]{:S(2)}) collective-permute-start(f32[4,128,128]{2,1,0:T(8,128)} %convert_add_fusion), channel_id=1, source_target_pairs={{0,128},{8,136},{16,144},{24,152},{32,160},{40,168},{48,176},{56,1... | collective-permute-start | bytes 786440 | tf_op jit(solution)/shard_map/ppermute | solution.py:24
  205.3 11.9 %collective-permute-start.9 = (f32[4,128,128]{2,1,0:T(8,128)}, f32[4,128,128]{2,1,0:T(8,128)}, u32[]{:S(2)}, u32[]{:S(2)}) collective-permute-start(f32[4,128,128]{2,1,0:T(8,128)} %convert_add_fusion), channel_id=1, source_target_pairs={{0,192},{8,200},{16,208},{24,216},{32,224},{40,232},{48,240},{56,2... | collective-permute-start | bytes 786440 | tf_op jit(solution)/shard_map/ppermute | solution.py:24
  218.5 1.2 copy-start.3
  219.7 0.7 copy-start.5
Sparse Core Ops, SparseCore 0:
  9.2 37.4 all-gather.1
  227.6 35.1 reduce-scatter.1
where the time goes:
time: 272 us; the launch traced here: 270 us
  other arithmetic  133 us (49%)
  waiting for transfers between devices  60.6 us (22%)
  starting transfers between devices  21.8 us (8%)
  matrix products  20.4 us (7%)
  local copies, waits for them, and re-layouts  20 us (7%)
  between operations  14 us (5%)
    convert_element_type x12, other arithmetic, project(): blocks_out.append(summed.astype(jnp.bfloat16))  124 us
    reduce_scatter x1, waiting for transfers between devices, on_device(): lax.psum_scatter(partial_value.astype(jnp.bfloat16), 'tp', scatter_dimens...  35.3 us
    ppermute x10, starting transfers between devices, ring_gather(): got = lax.ppermute(value, axis, pairs).astype(jnp.float32)  21.8 us
    all_gather x1, waiting for transfers between devices, on_device(): whole = lax.all_gather(tokens, 'tp', axis=1, tiled=True)  16.5 us
    dot_general x8, matrix products, project(): jnp.dot(whole[:, c * rows:(c + 1) * rows], weights, preferred_element_typ...  10.7 us
    unnamed x19, local copies, waits for them, and re-layouts  9.4 us
    ppermute x10, waiting for transfers between devices, ring_gather(): got = lax.ppermute(value, axis, pairs).astype(jnp.float32)  8.1 us
    slice x11, local copies, waits for them, and re-layouts, project(): part = products[c][:, at:at + cols] * mixing[p, term_index, c, r]  7.7 us
  transfers between devices with their start and end apart: 12, of which 5 were waited for; matrix products, arithmetic and copies ran while one was open for 26% of the time, Pallas kernels for 0%

commit v1 on v0

--- a/solution.py
+++ b/solution.py
@@ -9,6 +9,13 @@
 HEAD = 128
 BLOCK = 1024
 epsilon = 1e-06
+
+
+def put_tracks_in(arr):
+    nodes = lax.axis_size("tp")
+    block_next = jnp.tile(arr, [nodes if idx == 1 else 1 for idx in range(arr.ndim)])
+    then = lax.all_to_all(block_next, "tp", split_axis=1, concat_axis=1, tiled=True)
+    return then
 
 
 def ring_gather(value, axis, devices, size, stride, before):
@@ -74,7 +81,7 @@
 def on_device(ctx_devices, ctx_row, tokens, qkv_blocks, out_blocks, mix_factors, head_gain):
     col_width = qkv_blocks.shape[-1]
     w_out = fold_weights(out_blocks, mix_factors[3]).astype(jnp.bfloat16)
-    whole = lax.all_gather(tokens, "tp", axis=1, tiled=True)
+    whole = put_tracks_in(tokens)
     tok_rows = whole.shape[0]
     local_heads = PHM * col_width // HEAD
     nblk = tok_rows // SPAN

time: 272 us -> 297 us (1.092)
  local copies, waits for them, and re-layouts: 20 us -> 30.1 us
  waiting for transfers between devices: 60.6 us -> 69.9 us
  starting transfers between devices: 21.8 us -> 28 us
    all_to_all x0 -> x1, waiting for transfers between devices: none -> 26.8 us  [put_tracks_in(): lax.all_to_all(block_next, 'tp', split_axis=1, concat_axis=1, tiled=True)]
    all_gather x1 -> x0, waiting for transfers between devices: 16.5 us -> none  [on_device(): whole = lax.all_gather(tokens, 'tp', axis=1, tiled=True)]
    all_to_all x0 -> x1, local copies, waits for them, and re-layouts: none -> 6.51 us  [put_tracks_in(): lax.all_to_all(block_next, 'tp', split_axis=1, concat_axis=1, tiled=True)]
    all_to_all x0 -> x1, starting transfers between devices: none -> 4.57 us  [put_tracks_in(): lax.all_to_all(block_next, 'tp', split_axis=1, concat_axis=1, tiled=True)]
    another operation x0 -> x1, local copies, waits for them, and re-layouts: none -> 3.4 us  [put_tracks_in(): jnp.tile(arr, [nodes if idx == 1 else 1 for idx in range(arr.ndim)])]
  transfers between devices with their start and end apart: 12 -> 12, of which waited for: 5 -> 5; matrix products, arithmetic and copies ran while one was open for 26% -> 23% of each run, Pallas kernels for 0% -> 0%
where the time goes in v1:
time: 297 us; the launch traced here: 295 us
  other arithmetic  133 us (45%)
  waiting for transfers between devices  69.9 us (24%)
  local copies, waits for them, and re-layouts  30.1 us (10%)
  starting transfers between devices  28 us (9%)
  matrix products  20.3 us (7%)
  between operations  14 us (5%)
    convert_element_type x12, other arithmetic, project(): blocks_out.append(summed.astype(jnp.bfloat16))  124 us
    reduce_scatter x1, waiting for transfers between devices, on_device(): lax.psum_scatter(partial_value.astype(jnp.bfloat16), 'tp', scatter_dimens...  35.9 us
    all_to_all x1, waiting for transfers between devices, put_tracks_in(): lax.all_to_all(block_next, 'tp', split_axis=1, concat_axis=1, tiled=True)  26.8 us
    ppermute x10, starting transfers between devices, ring_gather(): got = lax.ppermute(value, axis, pairs).astype(jnp.float32)  23.4 us
    dot_general x8, matrix products, project(): jnp.dot(whole[:, c * rows:(c + 1) * rows], weights, preferred_element_typ...  10.6 us
    unnamed x19, local copies, waits for them, and re-layouts  9.45 us
    slice x11, local copies, waits for them, and re-layouts, project(): part = products[c][:, at:at + cols] * mixing[p, term_index, c, r]  7.75 us
    ppermute x10, waiting for transfers between devices, ring_gather(): got = lax.ppermute(value, axis, pairs).astype(jnp.float32)  7.19 us
  transfers between devices with their start and end apart: 12, of which 5 were waited for; matrix products, arithmetic and copies ran while one was open for 23% of the time, Pallas kernels for 0%

profile of v1, /device:TPU:8, one launch (start us, length us, event | category | flops | bytes accessed | tf_op | source)
XLA Modules:
  0.0 295.2 jit_solution(10481345619869007094)
XLA Ops:
  6.5 3.4 %tile.2 = bf16[512,8,512]{2,0,1:T(8,128)(2,1)} broadcast(bf16[512,512]{1,0:T(8,128)(2,1)} %param.5), dimensions={0,2} | broadcast | bytes 4718592 | tf_op jit(solution)/shard_map/tile | solution.py:16
  9.9 4.6 %all-to-all-start = ((bf16[512,8,512]{2,0,1:T(8,128)(2,1)}), bf16[512,8,512]{2,0,1:T(8,128)(2,1)}, u32[]{:S(2)}, u32[]{:S(2)}) async-start(bf16[512,8,512]{2,0,1:T(8,128)(2,1)} %tile.2), calls=%async_computation | async-start | bytes 8388608 | tf_op jit(solution)/shard_map/all_to_all | solution.py:17
  14.8 1.6 slice-done
  16.3 2.8 copy.45
  19.1 1.3 copy.46
  20.7 4.6 %add_convert_fusion = bf16[4,128,4,1024]{3,2,1,0:T(4,128)(2,1)S(1)} fusion(f32[128,1024]{1,0:T(8,128)S(1)} %get-tuple-element.15, f32[4,4]{1,0:T(4,128)S(1)} %get-tuple-element.212, f32[128,1024]{1,0:T(8,128)S(1)} %get-tuple-element.16, f32[4,4]{1,0:T(4,128)S(1)} %get-tuple-element.211, f32[128,1024]{1,0:T(8,128)S(1)} %get-tuple-element.14, ...), kind=kLoop, calls=%fused_computation | loop fusion | flops 16777216 | bytes 6291712 | tf_op jit(solution)/shard_map/convert_element_type | solution.py:83
  25.3 4.2 %copy.48 = bf16[64,8,4,1024]{3,1,2,0:T(8,128)(2,1)} copy(bf16[64,8,4,1024]{3,2,1,0:T(4,128)(2,1)S(1)} %bitcast.276) | data formatting | bytes 8388608
  29.6 0.6 fusion.59
  30.2 0.6 fusion.57
  30.8 0.7 fusion.49
  31.6 0.7 fusion.50
  32.3 0.7 fusion.51
  33.0 0.7 fusion.52
  33.7 0.7 fusion.53
  34.5 0.7 fusion.54
  35.2 0.7 fusion.56
  35.9 0.7 fusion.55
  36.6 0.7 fusion.58
  37.4 26.8 %all-to-all-done = bf16[512,8,512]{2,0,1:T(8,128)(2,1)} async-done(((bf16[512,8,512]{2,0,1:T(8,128)(2,1)}), bf16[512,8,512]{2,0,1:T(8,128)(2,1)}, u32[]{:S(2)}, u32[]{:S(2)}) %all-to-all-start) | async-done | bytes 4194336 | tf_op jit(solution)/shard_map/all_to_all | solution.py:17
  64.2 6.5 %copy.32 = bf16[512,8,512]{0,2,1:T(8,128)(2,1)} copy(bf16[512,8,512]{2,0,1:T(8,128)(2,1)} %all-to-all-done) | data formatting | bytes 8388608 | tf_op jit(solution)/shard_map/all_to_all | solution.py:17
  70.7 2.7 fusion.11
  73.4 1.3 fusion.15
  74.7 1.3 fusion.19
  76.0 1.3 fusion.23
  77.3 10.2 %add_convert_fusion.8 = bf16[512,128]{1,0:T(8,128)(2,1)S(1)} fusion(f32[512,1024]{1,0:T(8,128)S(1)} %fusion.11, f32[512,1024]{1,0:T(8,128)S(1)} %fusion.15, f32[512,1024]{1,0:T(8,128)S(1)} %fusion.19, f32[512,1024]{1,0:T(8,128)S(1)} %fusion.23, f32[]{:T(128)} %bitcast.83, f32[]{:T(128)} %bitcast.82, f32[]{:T(128)} %bitcast.81, f32[]{:T(128)} %bitcast.80, ...), kind=kLoop, calls=%fused_computation.83 | loop fusion | flops 2097152 | bytes 4325440 | tf_op jit(solution)/shard_map/convert_element_type | solution.py:76
  87.5 10.2 %add_convert_fusion.7 = bf16[512,128]{1,0:T(8,128)(2,1)S(1)} fusion(f32[512,1024]{1,0:T(8,128)S(1)} %fusion.11, f32[512,1024]{1,0:T(8,128)S(1)} %fusion.15, f32[512,1024]{1,0:T(8,128)S(1)} %fusion.19, f32[512,1024]{1,0:T(8,128)S(1)} %fusion.23, f32[]{:T(128)} %bitcast.99, f32[]{:T(128)} %bitcast.98, f32[]{:T(128)} %bitcast.97, f32[]{:T(128)} %bitcast.96, ...), kind=kLoop, calls=%fused_computation.82 | loop fusion | flops 2097152 | bytes 4325440 | tf_op jit(solution)/shard_map/convert_element_type | solution.py:76
  97.7 10.2 %add_convert_fusion.6 = bf16[512,128]{1,0:T(8,128)(2,1)S(1)} fusion(f32[512,1024]{1,0:T(8,128)S(1)} %fusion.11, f32[512,1024]{1,0:T(8,128)S(1)} %fusion.15, f32[512,1024]{1,0:T(8,128)S(1)} %fusion.19, f32[512,1024]{1,0:T(8,128)S(1)} %fusion.23, f32[]{:T(128)} %bitcast.115, f32[]{:T(128)} %bitcast.114, f32[]{:T(128)} %bitcast.113, f32[]{:T(128)} %bitcast.112, ...), kind=kLoop, calls=%fused_computation.81 | loop fusion | flops 2097152 | bytes 4325440 | tf_op jit(solution)/shard_map/convert_element_type | solution.py:76
  107.9 10.4 %add_convert_fusion.5 = bf16[512,128]{1,0:T(8,128)(2,1)S(1)} fusion(f32[512,1024]{1,0:T(8,128)S(1)} %fusion.11, f32[512,1024]{1,0:T(8,128)S(1)} %fusion.15, f32[512,1024]{1,0:T(8,128)S(1)} %fusion.19, f32[512,1024]{1,0:T(8,128)S(1)} %fusion.23, f32[]{:T(128)} %bitcast.131, f32[]{:T(128)} %bitcast.130, f32[]{:T(128)} %bitcast.129, f32[]{:T(128)} %bitcast.128, ...), kind=kLoop, calls=%fused_computation.80 | loop fusion | flops 2097152 | bytes 4325440 | tf_op jit(solution)/shard_map/convert_element_type | solution.py:76
  118.3 10.3 %add_convert_fusion.11 = bf16[512,128]{1,0:T(8,128)(2,1)S(1)} fusion(f32[512,1024]{1,0:T(8,128)S(1)} %fusion.11, f32[512,1024]{1,0:T(8,128)S(1)} %fusion.15, f32[512,1024]{1,0:T(8,128)S(1)} %fusion.19, f32[512,1024]{1,0:T(8,128)S(1)} %fusion.23, f32[]{:T(128)} %bitcast.35, f32[]{:T(128)} %bitcast.34, f32[]{:T(128)} %bitcast.33, f32[]{:T(128)} %bitcast.32, ...), kind=kLoop, calls=%fused_computation.86 | loop fusion | flops 2097152 | bytes 4325440 | tf_op jit(solution)/shard_map/convert_element_type | solution.py:76
  128.6 10.3 %add_convert_fusion.10 = bf16[512,128]{1,0:T(8,128)(2,1)S(1)} fusion(f32[512,1024]{1,0:T(8,128)S(1)} %fusion.11, f32[512,1024]{1,0:T(8,128)S(1)} %fusion.15, f32[512,1024]{1,0:T(8,128)S(1)} %fusion.19, f32[512,1024]{1,0:T(8,128)S(1)} %fusion.23, f32[]{:T(128)} %bitcast.51, f32[]{:T(128)} %bitcast.50, f32[]{:T(128)} %bitcast.49, f32[]{:T(128)} %bitcast.48, ...), kind=kLoop, calls=%fused_computation.85 | loop fusion | flops 2097152 | bytes 4325440 | tf_op jit(solution)/shard_map/convert_element_type | solution.py:76
  138.9 10.3 %add_convert_fusion.9 = bf16[512,128]{1,0:T(8,128)(2,1)S(1)} fusion(f32[512,1024]{1,0:T(8,128)S(1)} %fusion.11, f32[512,1024]{1,0:T(8,128)S(1)} %fusion.15, f32[512,1024]{1,0:T(8,128)S(1)} %fusion.19, f32[512,1024]{1,0:T(8,128)S(1)} %fusion.23, f32[]{:T(128)} %bitcast.67, f32[]{:T(128)} %bitcast.66, f32[]{:T(128)} %bitcast.65, f32[]{:T(128)} %bitcast.64, ...), kind=kLoop, calls=%fused_computation.84 | loop fusion | flops 2097152 | bytes 4325440 | tf_op jit(solution)/shard_map/convert_element_type | solution.py:76
  149.2 10.5 %add_convert_fusion.12 = bf16[512,128]{1,0:T(8,128)(2,1)S(1)} fusion(f32[512,1024]{1,0:T(8,128)S(1)} %fusion.11, f32[512,1024]{1,0:T(8,128)S(1)} %fusion.15, f32[512,1024]{1,0:T(8,128)S(1)} %fusion.19, f32[512,1024]{1,0:T(8,128)S(1)} %fusion.23, f32[]{:T(128)} %bitcast.19, f32[]{:T(128)} %bitcast.18, f32[]{:T(128)} %bitcast.17, f32[]{:T(128)} %bitcast.16, ...), kind=kLoop, calls=%fused_computation.87 | loop fusion | flops 2097152 | bytes 4325440 | tf_op jit(solution)/shard_map/convert_element_type | solution.py:76
  160.0 0.3 copy.38
  160.4 1.0 fusion.60
  161.4 1.9 collective-permute-start
  163.3 3.3 %collective-permute-start.1 = (bf16[4,128,128]{2,1,0:T(8,128)(2,1)}, bf16[4,128,128]{2,1,0:T(8,128)(2,1)S(1)}, u32[]{:S(2)}, u32[]{:S(2)}) collective-permute-start(bf16[4,128,128]{2,1,0:T(8,128)(2,1)} %get-tuple-element.213), channel_id=1, source_target_pairs={{0,16},{8,24},{16,32},{24,40},{32,48},{40,56},{48,0},{56,8},{64,80... | collective-permute-start | bytes 393224 | tf_op jit(solution)/shard_map/ppermute | solution.py:31
  166.6 4.0 %collective-permute-start.2 = (bf16[4,128,128]{2,1,0:T(8,128)(2,1)}, bf16[4,128,128]{2,1,0:T(8,128)(2,1)S(1)}, u32[]{:S(2)}, u32[]{:S(2)}) collective-permute-start(bf16[4,128,128]{2,1,0:T(8,128)(2,1)} %get-tuple-element.213), channel_id=1, source_target_pairs={{0,24},{8,32},{16,40},{24,48},{32,56},{40,0},{48,8},{56,16},{64,88... | collective-permute-start | bytes 393224 | tf_op jit(solution)/shard_map/ppermute | solution.py:31
  170.6 0.5 collective-permute-start.3
  171.1 4.9 %collective-permute-start.4 = (bf16[4,128,128]{2,1,0:T(8,128)(2,1)}, bf16[4,128,128]{2,1,0:T(8,128)(2,1)}, u32[]{:S(2)}, u32[]{:S(2)}) collective-permute-start(bf16[4,128,128]{2,1,0:T(8,128)(2,1)} %get-tuple-element.213), channel_id=1, source_target_pairs={{0,40},{8,48},{16,56},{24,0},{32,8},{40,16},{48,24},{56,32},{64,10... | collective-permute-start | bytes 393224 | tf_op jit(solution)/shard_map/ppermute | solution.py:31
  176.1 1.9 fusion.13
  178.0 0.7 fusion.17
  178.7 0.7 fusion.21
  179.5 0.7 fusion.9
  180.2 10.3 %add_convert_fusion.3 = bf16[512,128]{0,1:T(8,128)(2,1)S(1)} fusion(f32[512,512]{0,1:T(8,128)S(1)} %fusion.9, f32[512,512]{0,1:T(8,128)S(1)} %fusion.13, f32[512,512]{0,1:T(8,128)S(1)} %fusion.17, f32[512,512]{0,1:T(8,128)S(1)} %fusion.21, f32[]{:T(128)} %bitcast.166, f32[]{:T(128)} %bitcast.165, f32[]{:T(128)} %bitcast.164, f32[]{:T(128)} %bitcast.163, ...), kind=kLoop, calls=%fused_computation.78 | loop fusion | flops 2097152 | bytes 4325440 | tf_op jit(solution)/shard_map/convert_element_type | solution.py:76
  190.5 10.4 %add_convert_fusion.2 = bf16[512,128]{0,1:T(8,128)(2,1)S(1)} fusion(f32[512,512]{0,1:T(8,128)S(1)} %fusion.9, f32[512,512]{0,1:T(8,128)S(1)} %fusion.13, f32[512,512]{0,1:T(8,128)S(1)} %fusion.17, f32[512,512]{0,1:T(8,128)S(1)} %fusion.21, f32[]{:T(128)} %bitcast.182, f32[]{:T(128)} %bitcast.181, f32[]{:T(128)} %bitcast.180, f32[]{:T(128)} %bitcast.179, ...), kind=kLoop, calls=%fused_computation.77 | loop fusion | flops 2097152 | bytes 4325440 | tf_op jit(solution)/shard_map/convert_element_type | solution.py:76
  200.9 10.5 %add_convert_fusion.1 = bf16[512,128]{0,1:T(8,128)(2,1)S(1)} fusion(f32[512,512]{0,1:T(8,128)S(1)} %fusion.9, f32[512,512]{0,1:T(8,128)S(1)} %fusion.13, f32[512,512]{0,1:T(8,128)S(1)} %fusion.17, f32[512,512]{0,1:T(8,128)S(1)} %fusion.21, f32[]{:T(128)} %bitcast.198, f32[]{:T(128)} %bitcast.197, f32[]{:T(128)} %bitcast.196, f32[]{:T(128)} %bitcast.195, ...), kind=kLoop, calls=%fused_computation.76 | loop fusion | flops 2097152 | bytes 4325440 | tf_op jit(solution)/shard_map/convert_element_type | solution.py:76
  211.5 2.7 collective-permute-start.5
  214.2 1.0 collective-permute-start.6
  215.2 10.5 %add_convert_fusion.4 = bf16[512,128]{0,1:T(8,128)(2,1)S(1)} fusion(f32[512,512]{0,1:T(8,128)S(1)} %fusion.9, f32[512,512]{0,1:T(8,128)S(1)} %fusion.13, f32[512,512]{0,1:T(8,128)S(1)} %fusion.17, f32[512,512]{0,1:T(8,128)S(1)} %fusion.21, f32[]{:T(128)} %bitcast.150, f32[]{:T(128)} %bitcast.149, f32[]{:T(128)} %bitcast.148, f32[]{:T(128)} %bitcast.147, ...), kind=kLoop, calls=%fused_computation.79 | loop fusion | flops 2097152 | bytes 4325440 | tf_op jit(solution)/shard_map/convert_element_type | solution.py:76
  225.8 0.4 copy.35
  226.3 2.0 convert_add_fusion
  228.3 1.6 collective-permute-start.7
  229.9 0.9 collective-permute-start.8
  230.8 2.4 collective-permute-start.9
  233.2 1.6 fusion.2
  234.9 2.2 collective-permute-done.7
  237.1 2.9 collective-permute-done.8
  240.0 2.0 collective-permute-done.9
  242.0 1.3 fusion.44
  243.7 0.9 copy-done.5
  244.6 0.5 multiply_reduce_fusion
  245.5 0.3 copy.43
  245.8 6.6 %convolution_convert_fusion = bf16[512,4096]{1,0:T(8,128)(2,1)} fusion(bf16[512,4096]{1,0:T(8,128)(2,1)} %bitcast.277, bf16[64,8,4,128]{3,2,1,0:T(4,128)(2,1)S(1)} %bitcast.296), kind=kOutput, calls=%fused_computation.1 | convolution fusion | flops 2149580800 | bytes 8912896 | tf_op jit(solution)/shard_map/dot_general | solution.py:121
  252.4 35.9 %reduce-scatter.2.cloned.1.call-done = bf16[512,512]{1,0:T(8,128)(2,1)} async-done(((bf16[512,4096]{1,0:T(8,128)(2,1)}), bf16[512,512]{1,0:T(8,128)(2,1)}) %reduce-scatter.2.cloned.1.call-update) | async-done | bytes 524304 | tf_op jit(solution)/shard_map/reduce_scatter | solution.py:122
  (40 shorter events, 1.5 us)
Async XLA Ops:
  9.9 54.2 %all-to-all-start = ((bf16[512,8,512]{2,0,1:T(8,128)(2,1)}), bf16[512,8,512]{2,0,1:T(8,128)(2,1)}, u32[]{:S(2)}, u32[]{:S(2)}) async-start(bf16[512,8,512]{2,0,1:T(8,128)(2,1)} %tile.2), calls=%async_computation | async-start | bytes 8388608 | tf_op jit(solution)/shard_map/all_to_all | solution.py:17
  14.5 273.8 %reduce-scatter.2.cloned.1.call-start = ((), (), s32[]{:S(2)}) async-start(), calls=%async_computation.2 | async-start | bytes 4718592 | tf_op jit(solution)/shard_map/reduce_scatter | solution.py:122
  14.7 1.6 slice-start
  16.3 2.8 slice-start.1
  19.1 1.3 copy-start.6
  19.1 1.3 copy-start.3
  37.4 33.3 %copy-start.2 = (bf16[2,4,1024,128]{2,3,1,0:T(8,128)(2,1)S(1)}, bf16[2,4,1024,128]{2,3,1,0:T(8,128)(2,1)}, u32[]{:S(2)}) copy-start(bf16[2,4,1024,128]{2,3,1,0:T(8,128)(2,1)} %copy.45) | copy-start | bytes 6291460
  70.7 2.7 copy-start
  160.0 16.1 %copy-start.4 = (bf16[1,4,1024,128]{2,3,1,0:T(8,128)(2,1)S(1)}, bf16[1,4,1024,128]{2,3,1,0:T(8,128)(2,1)}, u32[]{:S(2)}) copy-start(bf16[1,4,1024,128]{2,3,1,0:T(8,128)(2,1)} %copy.46) | copy-start | bytes 3145732
  160.4 17.6 %copy-start.1 = (bf16[512,8,512]{0,2,1:T(8,128)(2,1)S(1)}, bf16[512,8,512]{0,2,1:T(8,128)(2,1)}, u32[]{:S(2)}) copy-start(bf16[512,8,512]{0,2,1:T(8,128)(2,1)} %copy.32) | copy-start | bytes 12582916
  161.4 50.1 %collective-permute-start = (bf16[4,128,128]{2,1,0:T(8,128)(2,1)}, bf16[4,128,128]{2,1,0:T(8,128)(2,1)S(1)}, u32[]{:S(2)}, u32[]{:S(2)}) collective-permute-start(bf16[4,128,128]{2,1,0:T(8,128)(2,1)} %get-tuple-element.213), channel_id=1, source_target_pairs={{0,8},{8,16},{16,24},{24,32},{32,40},{40,48},{48,56},{56,0},{64,72... | collective-permute-start | bytes 393224 | tf_op jit(solution)/shard_map/ppermute | solution.py:31
  163.3 50.9 %collective-permute-start.1 = (bf16[4,128,128]{2,1,0:T(8,128)(2,1)}, bf16[4,128,128]{2,1,0:T(8,128)(2,1)S(1)}, u32[]{:S(2)}, u32[]{:S(2)}) collective-permute-start(bf16[4,128,128]{2,1,0:T(8,128)(2,1)} %get-tuple-element.213), channel_id=1, source_target_pairs={{0,16},{8,24},{16,32},{24,40},{32,48},{40,56},{48,0},{56,8},{64,80... | collective-permute-start | bytes 393224 | tf_op jit(solution)/shard_map/ppermute | solution.py:31
  166.6 59.7 %collective-permute-start.2 = (bf16[4,128,128]{2,1,0:T(8,128)(2,1)}, bf16[4,128,128]{2,1,0:T(8,128)(2,1)S(1)}, u32[]{:S(2)}, u32[]{:S(2)}) collective-permute-start(bf16[4,128,128]{2,1,0:T(8,128)(2,1)} %get-tuple-element.213), channel_id=1, source_target_pairs={{0,24},{8,32},{16,40},{24,48},{32,56},{40,0},{48,8},{56,16},{64,88... | collective-permute-start | bytes 393224 | tf_op jit(solution)/shard_map/ppermute | solution.py:31
  170.6 55.6 %collective-permute-start.3 = (bf16[4,128,128]{2,1,0:T(8,128)(2,1)}, bf16[4,128,128]{2,1,0:T(8,128)(2,1)}, u32[]{:S(2)}, u32[]{:S(2)}) collective-permute-start(bf16[4,128,128]{2,1,0:T(8,128)(2,1)} %get-tuple-element.213), channel_id=1, source_target_pairs={{0,32},{8,40},{16,48},{24,56},{32,0},{40,8},{48,16},{56,24},{64,96... | collective-permute-start | bytes 393224 | tf_op jit(solution)/shard_map/ppermute | solution.py:31
  171.1 55.1 %collective-permute-start.4 = (bf16[4,128,128]{2,1,0:T(8,128)(2,1)}, bf16[4,128,128]{2,1,0:T(8,128)(2,1)}, u32[]{:S(2)}, u32[]{:S(2)}) collective-permute-start(bf16[4,128,128]{2,1,0:T(8,128)(2,1)} %get-tuple-element.213), channel_id=1, source_target_pairs={{0,40},{8,48},{16,56},{24,0},{32,8},{40,16},{48,24},{56,32},{64,10... | collective-permute-start | bytes 393224 | tf_op jit(solution)/shard_map/ppermute | solution.py:31
  211.5 14.8 %collective-permute-start.5 = (bf16[4,128,128]{2,1,0:T(8,128)(2,1)}, bf16[4,128,128]{2,1,0:T(8,128)(2,1)}, u32[]{:S(2)}, u32[]{:S(2)}) collective-permute-start(bf16[4,128,128]{2,1,0:T(8,128)(2,1)} %get-tuple-element.213), channel_id=1, source_target_pairs={{0,48},{8,56},{16,0},{24,8},{32,16},{40,24},{48,32},{56,40},{64,11... | collective-permute-start | bytes 393224 | tf_op jit(solution)/shard_map/ppermute | solution.py:31
  214.2 12.1 %collective-permute-start.6 = (bf16[4,128,128]{2,1,0:T(8,128)(2,1)}, bf16[4,128,128]{2,1,0:T(8,128)(2,1)}, u32[]{:S(2)}, u32[]{:S(2)}) collective-permute-start(bf16[4,128,128]{2,1,0:T(8,128)(2,1)} %get-tuple-element.213), channel_id=1, source_target_pairs={{0,56},{8,0},{16,8},{24,16},{32,24},{40,32},{48,40},{56,48},{64,12... | collective-permute-start | bytes 393224 | tf_op jit(solution)/shard_map/ppermute | solution.py:31
  228.3 8.8 %collective-permute-start.7 = (f32[4,128,128]{2,1,0:T(8,128)}, f32[4,128,128]{2,1,0:T(8,128)S(1)}, u32[]{:S(2)}, u32[]{:S(2)}) collective-permute-start(f32[4,128,128]{2,1,0:T(8,128)} %convert_add_fusion), channel_id=1, source_target_pairs={{0,64},{8,72},{16,80},{24,88},{32,96},{40,104},{48,112},{56,120},{... | collective-permute-start | bytes 786440 | tf_op jit(solution)/shard_map/ppermute | solution.py:31
  229.9 10.2 %collective-permute-start.8 = (f32[4,128,128]{2,1,0:T(8,128)}, f32[4,128,128]{2,1,0:T(8,128)S(1)}, u32[]{:S(2)}, u32[]{:S(2)}) collective-permute-start(f32[4,128,128]{2,1,0:T(8,128)} %convert_add_fusion), channel_id=1, source_target_pairs={{0,128},{8,136},{16,144},{24,152},{32,160},{40,168},{48,176},{56,1... | collective-permute-start | bytes 786440 | tf_op jit(solution)/shard_map/ppermute | solution.py:31
  230.8 11.2 %collective-permute-start.9 = (f32[4,128,128]{2,1,0:T(8,128)}, f32[4,128,128]{2,1,0:T(8,128)}, u32[]{:S(2)}, u32[]{:S(2)}) collective-permute-start(f32[4,128,128]{2,1,0:T(8,128)} %convert_add_fusion), channel_id=1, source_target_pairs={{0,192},{8,200},{16,208},{24,216},{32,224},{40,232},{48,240},{56,2... | collective-permute-start | bytes 786440 | tf_op jit(solution)/shard_map/ppermute | solution.py:31
  243.4 1.2 copy-start.5
  244.6 0.7 copy-start.7
Sparse Core Ops, SparseCore 0:
  252.5 35.7 reduce-scatter.1
